TPU v7x, 128 devices: a whole 4x4x4 slice. The times are simulated.
128 devices in a mesh: row: 8 (over x, core), col: 4 (over z), depth: 4 (over y).
Axes of the slice: x: 4, y: 4, z: 4, core: 2. Of those that a mesh axis runs over, the one named last changes fastest.
Arguments:
- tokens: bfloat16 [1024, 8192], P(('col', 'depth'), 'row'), may hold values from -6 to 6
- gate_weight: bfloat16 [8192, 14336], P('row', ('col', 'depth')), may hold values from -0.109375 to 0.109375
- up_weight: bfloat16 [8192, 14336], P('row', ('col', 'depth')), may hold values from -0.109375 to 0.109375
- down_weight: bfloat16 [14336, 8192], P(('col', 'depth'), 'row'), may hold values from -0.078125 to 0.078125
- gate_mask: int32 [64, 112], P('row', ('col', 'depth')), may hold values 0 or 1
- up_mask: int32 [64, 112], P('row', ('col', 'depth')), may hold values 0 or 1
- down_mask: int32 [112, 64], P(('col', 'depth'), 'row'), may hold values 0 or 1
- grad_out: bfloat16 [1024, 8192], P(('col', 'depth'), 'row'), may hold values from -1.5 to 1.5
Outputs:
- mixed: bfloat16 [1024, 8192], P(('col', 'depth'), 'row')
- grad_tokens: bfloat16 [1024, 8192], P(('col', 'depth'), 'row')
- grad_gate_weight: bfloat16 [8192, 14336], P('row', ('col', 'depth'))
- grad_up_weight: bfloat16 [8192, 14336], P('row', ('col', 'depth'))
- grad_down_weight: bfloat16 [14336, 8192], P(('col', 'depth'), 'row')
Inputs may be any that keep to these rules, and one draw needn't show every extreme that they name: `gate_mask`: 1 keeps the 128 x 128 block of the gate projection, 0 zeroes it. `up_mask`: 1 keeps the 128 x 128 block of the up projection, 0 zeroes it. `down_mask`: 1 keeps the 128 x 128 block of the down projection, 0 zeroes it.
All inputs are finite; a program needn't handle non-finite values.
Results may differ from a plain program's by a relative error of at most 0.015.
Values may be sent and summed in bfloat16 or wider, within the bound.
No kernel may reach another device: no remote copies, remote signals or barrier semaphores. Data moves between devices by JAX's collectives and lax.ppermute only.
A program may use at most 128 MiB of HBM per device.

v0:
```python
import jax
import jax.numpy as jnp
from jax import lax
from jax.sharding import PartitionSpec as P

BLK = 128


def expand(mask):
    return jnp.repeat(jnp.repeat(mask, BLK, axis=0), BLK, axis=1) > 0


def swiglu(sums):
    width = sums.shape[1] // 2
    gate = sums[:, :width]
    up = sums[:, width:]
    sig = jax.nn.sigmoid(gate)
    return (gate * sig * up).astype(jnp.bfloat16)


def swiglu_back(sums, grad_act):
    width = sums.shape[1] // 2
    gate = sums[:, :width]
    up = sums[:, width:]
    sig = jax.nn.sigmoid(gate)
    grad_gate = grad_act * up * sig * (1.0 + gate * (1.0 - sig))
    grad_up = grad_act * gate * sig
    return jnp.concatenate([grad_gate, grad_up], axis=1).astype(jnp.bfloat16)


def row_sums(term, rows):
    return lax.psum_scatter(
        term(jnp.int32(0), lax.axis_size("row") * rows), "row", scatter_dimension=0, tiled=True
    )


def row_gather(block):
    return lax.all_gather(block, "row", axis=0, tiled=True)


def row_sums_direct(full):
    parts = lax.axis_size("row")
    rows = full.shape[0] // parts
    pieces = lax.all_to_all(
        full.astype(jnp.bfloat16).reshape((parts, rows) + full.shape[1:]), "row", 0, 0
    )
    return jnp.sum(pieces.astype(jnp.float32), axis=0)


def row_sums_paired(full):
    parts = lax.axis_size("row")
    chips = parts // 2
    rows = full.shape[0] // parts
    member = lax.axis_index("row")
    core = member % 2
    chip = member // 2
    blocks = full.reshape((chips, 2, rows) + full.shape[1:])
    give = jnp.take(blocks, 1 - core, axis=1)
    keep = jnp.take(blocks, core, axis=1)
    moved_in = lax.ppermute(give.astype(jnp.bfloat16), "row", [(i, i ^ 1) for i in range(parts)])
    pair = keep + moved_in.astype(jnp.float32)
    sent = pair.astype(jnp.bfloat16)
    total = jnp.take(pair, chip, axis=0)
    for hop in range(1, chips):
        piece = jnp.take(sent, (chip + hop) % chips, axis=0)
        moved = lax.ppermute(piece, "row", [(i, (i + 2 * hop) % parts) for i in range(parts)])
        total = total + moved.astype(jnp.float32)
    return total


def row_gather_direct(block):
    parts = lax.axis_size("row")
    copies = jnp.broadcast_to(block[None], (parts,) + block.shape)
    pieces = lax.all_to_all(copies, "row", 0, 0)
    return pieces.reshape((parts * block.shape[0],) + block.shape[1:])


def group_sums(term, rows):
    parts = lax.axis_size(("col", "depth"))
    full = term(jnp.int32(0), rows * parts).astype(jnp.bfloat16)
    pieces = lax.all_to_all(full.reshape((parts, rows) + full.shape[1:]), ("col", "depth"), 0, 0)
    return jnp.sum(pieces.astype(jnp.float32), axis=0)


def group_gather(block):
    parts = lax.axis_size(("col", "depth"))
    copies = jnp.broadcast_to(block[None], (parts,) + block.shape)
    pieces = lax.all_to_all(copies, ("col", "depth"), 0, 0)
    return pieces.reshape((parts * block.shape[0],) + block.shape[1:])


def local(tokens, gate_weight, up_weight, down_weight, gate_mask, up_mask, down_mask, grad_out):
    zero_value = jnp.zeros((), jnp.bfloat16)
    keep_gate = expand(gate_mask)
    keep_up = expand(up_mask)
    keep_down = expand(down_mask)
    w_both = jnp.concatenate(
        [jnp.where(keep_gate, gate_weight, zero_value), jnp.where(keep_up, up_weight, zero_value)],
        axis=1,
    )
    w_down = jnp.where(keep_down, down_weight, zero_value)
    x_all = group_gather(tokens)
    split_rows = x_all.shape[0] // lax.axis_size("row")
    own_rows = tokens.shape[0]
    inner = (((0,), (0,)), ((), ()))
    outer = (((1,), (1,)), ((), ()))
    hidden = jnp.dot(x_all, w_both, preferred_element_type=jnp.float32)
    sums = row_sums(lambda start, count: hidden, split_rows)
    grad_out, _ = lax.optimization_barrier((grad_out, hidden))
    grad_all = group_gather(grad_out)
    act_partial = lax.dot_general(grad_all, w_down, outer, preferred_element_type=jnp.float32)
    act_sums, act_partial = lax.optimization_barrier((sums, act_partial))
    act_all = row_gather(swiglu(act_sums))

    def out_term(start, count):
        return jnp.dot(act_all, w_down, preferred_element_type=jnp.float32)

    mixed = group_sums(out_term, own_rows).astype(jnp.bfloat16)
    grad_down = lax.dot_general(act_all, grad_all, inner, preferred_element_type=jnp.float32)
    grad_down_weight = jnp.where(keep_down, grad_down, jnp.float32(0.0)).astype(jnp.bfloat16)
    grad_act = row_sums_paired(act_partial)
    held_sums, grad_act, _ = lax.optimization_barrier((sums, grad_act, act_all))
    grads_all = row_gather(swiglu_back(held_sums, grad_act))
    grad_both = lax.dot_general(x_all, grads_all, inner, preferred_element_type=jnp.float32)
    width = grad_both.shape[1] // 2
    grad_gate_weight = jnp.where(keep_gate, grad_both[:, :width], jnp.float32(0.0)).astype(
        jnp.bfloat16
    )
    grad_up_weight = jnp.where(keep_up, grad_both[:, width:], jnp.float32(0.0)).astype(jnp.bfloat16)

    def input_term(start, count):
        return lax.dot_general(grads_all, w_both, outer, preferred_element_type=jnp.float32)

    grad_tokens = group_sums(input_term, own_rows).astype(jnp.bfloat16)
    return (mixed, grad_tokens, grad_gate_weight, grad_up_weight, grad_down_weight)


def solution(mesh):
    return jax.shard_map(
        local,
        mesh=mesh,
        in_specs=(
            P(("col", "depth"), "row"),
            P("row", ("col", "depth")),
            P("row", ("col", "depth")),
            P(("col", "depth"), "row"),
            P("row", ("col", "depth")),
            P("row", ("col", "depth")),
            P(("col", "depth"), "row"),
            P(("col", "depth"), "row"),
        ),
        out_specs=(
            P(("col", "depth"), "row"),
            P(("col", "depth"), "row"),
            P("row", ("col", "depth")),
            P("row", ("col", "depth")),
            P(("col", "depth"), "row"),
        ),
        check_vma=False,
    )
```

profile of v0, /device:TPU:1, one launch (start us, length us, event | category | flops | bytes accessed | tf_op | source)
XLA Modules:
  0.0 234.1 jit_solution(18047022158019151847)
XLA Ops:
  7.2 2.5 %broadcast_in_dim.83 = bf16[16,64,1024]{2,1,0:T(8,128)(2,1)} broadcast(bf16[64,1024]{1,0:T(8,128)(2,1)} %param.12), dimensions={1,2} | broadcast | bytes 2228224 | tf_op jit(solution)/shard_map/broadcast_in_dim | solution.py:87
  9.7 8.8 %all-to-all-start = ((bf16[16,64,1024]{2,1,0:T(8,128)(2,1)}), bf16[16,64,1024]{2,1,0:T(8,128)(2,1)}, u32[]{:S(2)}, u32[]{:S(2)}) async-start(bf16[16,64,1024]{2,1,0:T(8,128)(2,1)} %broadcast_in_dim.83), calls=%async_computation | async-start | bytes 4194304 | tf_op jit(solution)/shard_map/all_to_all | solution.py:88
  18.5 0.0 reduce-scatter.2.cloned.1.call-start
  18.5 0.0 copy-done.4
  18.5 0.1 copy.19
  18.6 0.0 copy-done.5
  18.6 0.1 copy.21
  18.7 0.1 broadcast_bitcast_fusion
  18.8 0.1 broadcast_bitcast_fusion.1
  18.9 2.9 %copy.20 = bf16[1024,896]{0,1:T(8,128)(2,1)S(1)} copy(bf16[1024,896]{1,0:T(8,128)(2,1)} %param.13) | data formatting | bytes 3670016 | tf_op args[1]
  21.8 3.8 %copy.22 = bf16[1024,896]{0,1:T(8,128)(2,1)} copy(bf16[1024,896]{1,0:T(8,128)(2,1)} %param.14) | data formatting | bytes 3670016 | tf_op args[2]
  25.6 3.6 %bitcast_select_fusion.1 = (bf16[1024,896]{0,1:T(8,128)(2,1)}, bf16[1024,896]{0,1:T(8,128)(2,1)}) fusion(bf16[1024,896]{0,1:T(8,128)(2,1)} %copy.22, pred[1024,7]{0,1:T(8,128)(4,1)S(1)} %bitcast.75, bf16[1024,896]{0,1:T(8,128)(2,1)S(1)} %copy.20, pred[1024,7]{0,1:T(8,128)(4,1)S(1)} %bitcast.77), kind=kLoop, calls=%fused_computation.1 | loop fusion | flops 1835008 | bytes 7354368 | tf_op jit(solution)/shard_map/jit(_where)/select_n | solution.py:98
  29.2 20.2 %all-to-all-done = bf16[16,64,1024]{2,1,0:T(8,128)(2,1)} async-done(((bf16[16,64,1024]{2,1,0:T(8,128)(2,1)}), bf16[16,64,1024]{2,1,0:T(8,128)(2,1)}, u32[]{:S(2)}, u32[]{:S(2)}) %all-to-all-start) | async-done | bytes 2097184 | tf_op jit(solution)/shard_map/all_to_all | solution.py:88
  49.5 9.7 %convolution_bitcast_fusion.1 = f32[1024,1792]{0,1:T(8,128)} fusion(bf16[1024,1024]{1,0:T(8,128)(2,1)} %bitcast.2, bf16[1024,896]{0,1:T(8,128)(2,1)} %get-tuple-element.69, bf16[1024,896]{0,1:T(8,128)(2,1)} %get-tuple-element.70), kind=kOutput, calls=%fused_computation.5 | convolution fusion | flops 3765436416 | bytes 13107200 | tf_op jit(solution)/shard_map/dot_general | solution.py:107
  59.1 0.0 reduce-scatter.2.cloned.1.call-update
  59.1 0.9 copy-done.3
  60.0 1.7 broadcast_in_dim.84
  61.7 3.9 %all-to-all-start.1 = ((bf16[16,64,1024]{2,1,0:T(8,128)(2,1)}), bf16[16,64,1024]{2,1,0:T(8,128)(2,1)S(1)}, u32[]{:S(2)}, u32[]{:S(2)}) async-start(bf16[16,64,1024]{2,1,0:T(8,128)(2,1)} %broadcast_in_dim.84), calls=%async_computation.2 | async-start | bytes 4194304 | tf_op jit(solution)/shard_map/all_to_all | solution.py:88
  65.6 0.0 all-gather.3.cloned.1.call-start
  65.7 0.0 copy-done.6
  65.7 28.5 %all-to-all-done.1 = bf16[16,64,1024]{2,1,0:T(8,128)(2,1)S(1)} async-done(((bf16[16,64,1024]{2,1,0:T(8,128)(2,1)}), bf16[16,64,1024]{2,1,0:T(8,128)(2,1)S(1)}, u32[]{:S(2)}, u32[]{:S(2)}) %all-to-all-start.1) | async-done | bytes 2097184 | tf_op jit(solution)/shard_map/all_to_all | solution.py:88
  94.3 2.8 %broadcast_in_dim.86 = pred[896,8,128]{2,1,0:T(8,128)(4,1)S(1)} broadcast(pred[896,8]{1,0:T(8,128)(4,1)S(1)} %bitcast.74), dimensions={0,1} | broadcast | bytes 924672 | tf_op jit(solution)/shard_map/broadcast_in_dim | solution.py:10
  97.1 5.9 %fusion.4 = f32[1024,896]{1,0:T(8,128)} fusion(bf16[1024,1024]{1,0:T(8,128)(2,1)S(1)} %bitcast.65, bf16[896,1024]{1,0:T(8,128)(2,1)} %param.15, pred[112,8,8,128]{3,2,1,0:T(8,128)(4,1)S(1)} %bitcast.71), kind=kOutput, calls=%fused_computation.16 | convolution fusion | flops 1879965696 | bytes 8519680 | tf_op jit(solution)/shard_map/dot_general | solution.py:111
  103.0 0.0 copy-done.2
  103.0 2.1 reduce-scatter.2.cloned.1.call-done
  105.1 2.0 multiply_convert_fusion.2
  107.1 0.0 all-gather.3.cloned.1.call-update
  107.1 0.0 all-gather.5.cloned.1.call-start
  107.2 1.6 constant_dynamic-slice_fusion
  108.8 0.6 copy.28
  109.4 1.1 bitcast_convert_fusion
  110.6 1.2 collective-permute-start
  111.8 2.8 %constant_dynamic-slice_fusion.1 = f32[4,1,128,896]{3,2,1,0:T(8,128)} fusion(f32[4,2,128,896]{3,2,1,0:T(8,128)} %bitcast.70, s32[]{:T(128)S(6)} %select_n.92), kind=kLoop, calls=%fused_computation.38 | loop fusion | bytes 3670020 | tf_op jit(solution)/shard_map/jit(_take) | solution.py:59
  114.6 1.8 copy.27
  116.4 0.0 collective-permute-done
  116.4 2.7 %fusion.13 = (bf16[4,128,896]{1,2,0:T(8,128)(2,1)S(1)}, f32[4,128,896]{1,2,0:T(8,128)}) fusion(bf16[4,128,896]{1,2,0:T(8,128)(2,1)} %collective-permute-done, f32[4,1,128,896]{2,3,0,1:T(8,128)S(1)} %copy.27, pred[]{:T(512)S(6)} %and.48), kind=kLoop, calls=%fused_computation.43 | loop fusion | flops 1835008 | bytes 5505025 | tf_op jit(solution)/shard_map/convert_element_type | solution.py:62
  119.1 0.1 select_bitcast_fusion.2
  119.2 1.1 collective-permute-start.1
  120.3 1.7 collective-permute-start.3
  121.9 1.3 collective-permute-start.2
  123.3 7.4 %collective-permute-done.1 = bf16[128,896]{0,1:T(8,128)(2,1)S(1)} collective-permute-done((bf16[128,896]{0,1:T(8,128)(2,1)S(1)}, bf16[128,896]{0,1:T(8,128)(2,1)S(1)}, u32[]{:S(2)}, u32[]{:S(2)}) %collective-permute-start.1) | collective-permute-done | bytes 229408 | tf_op jit(solution)/shard_map/ppermute | solution.py:66
  130.7 0.0 collective-permute-done.3
  130.7 7.5 %collective-permute-done.2 = bf16[128,896]{0,1:T(8,128)(2,1)S(1)} collective-permute-done((bf16[128,896]{0,1:T(8,128)(2,1)S(1)}, bf16[128,896]{0,1:T(8,128)(2,1)S(1)}, u32[]{:S(2)}, u32[]{:S(2)}) %collective-permute-start.2) | collective-permute-done | bytes 229408 | tf_op jit(solution)/shard_map/ppermute | solution.py:66
  138.3 1.1 fusion.8
  139.4 0.0 all-gather.3.cloned.1.call-done
  139.4 0.0 copy-done.1
  139.4 0.2 multiply_convert_fusion.1
  139.7 0.8 pad_maximum_fusion.5
  140.5 0.0 all-gather.5.cloned.1.call-update
  140.5 5.8 %convolution_convert_fusion = bf16[1024,1024]{1,0:T(8,128)(2,1)} fusion(bf16[1024,896]{0,1:T(8,128)(2,1)} %all-gather.3.cloned.1.call-done, bf16[896,1024]{1,0:T(8,128)(2,1)} %param.15, pred[112,8,8,128]{3,2,1,0:T(8,128)(4,1)S(1)} %bitcast.72), kind=kOutput, calls=%fused_computation.13 | convolution fusion | flops 1881014272 | bytes 6684672 | tf_op jit(solution)/shard_map/dot_general | solution.py:116
  146.3 7.7 %all-to-all-start.2 = ((bf16[16,64,1024]{2,1,0:T(8,128)(2,1)}), bf16[16,64,1024]{2,1,0:T(8,128)(2,1)S(1)}, u32[]{:S(2)}, u32[]{:S(2)}) async-start(bf16[16,64,1024]{2,1,0:T(8,128)(2,1)} %bitcast.68), calls=%async_computation.3 | async-start | bytes 4194304 | tf_op jit(solution)/shard_map/all_to_all | solution.py:81
  154.1 23.3 %all-gather.5.cloned.1.call-done = bf16[1024,1792]{0,1:T(8,128)(2,1)} async-done(((bf16[128,1792]{0,1:T(8,128)(2,1)}), bf16[1024,1792]{0,1:T(8,128)(2,1)}) %all-gather.5.cloned.1.call-update) | async-done | bytes 3670032 | tf_op jit(solution)/shard_map/all_gather | solution.py:38
  177.4 8.5 %fusion.3 = bf16[1024,1024]{1,0:T(8,128)(2,1)} fusion(bf16[1024,1792]{0,1:T(8,128)(2,1)} %all-gather.5.cloned.1.call-done, bf16[1024,896]{0,1:T(8,128)(2,1)} %get-tuple-element.69, bf16[1024,896]{0,1:T(8,128)(2,1)} %get-tuple-element.70), kind=kOutput, calls=%fused_computation.12 | convolution fusion | flops 3766484992 | bytes 9437184 | tf_op jit(solution)/shard_map/dot_general | solution.py:132
  185.9 0.8 all-to-all-done.2
  186.7 1.3 copy-done
  188.0 5.9 %all-to-all-start.3 = ((bf16[16,64,1024]{2,1,0:T(8,128)(2,1)}), bf16[16,64,1024]{2,1,0:T(8,128)(2,1)S(1)}, u32[]{:S(2)}, u32[]{:S(2)}) async-start(bf16[16,64,1024]{2,1,0:T(8,128)(2,1)} %bitcast.67), calls=%async_computation.4 | async-start | bytes 4194304 | tf_op jit(solution)/shard_map/all_to_all | solution.py:81
  193.9 5.5 %select_convert_fusion = bf16[896,1024]{1,0:T(8,128)(2,1)} fusion(pred[112,8,8,128]{3,2,1,0:T(8,128)(4,1)S(1)} %bitcast.73, bf16[1024,896]{0,1:T(8,128)(2,1)} %all-gather.3.cloned.1.call-done, bf16[1024,1024]{1,0:T(8,128)(2,1)} %bitcast.66), kind=kOutput, calls=%fused_computation.9 | convolution fusion | flops 1880883200 | bytes 6684672 | tf_op jit(solution)/shard_map/dot_general | solution.py:119
  199.4 2.7 %reduce_sum.24 = bf16[64,1024]{1,0:T(8,128)(2,1)} reduce(bf16[16,64,1024]{2,1,0:T(8,128)(2,1)} %copy-done, bf16[]{:T(256)} %constant.84.clone.1), dimensions={0}, to_apply=%region_1.2 | reduce | flops 983040 | bytes 2228226 | tf_op jit(solution)/shard_map/reduce_sum | solution.py:82
  202.1 6.7 %convolution_bitcast_fusion = bf16[1024,1792]{0,1:T(8,128)(2,1)S(1)} fusion(bf16[1024,1792]{0,1:T(8,128)(2,1)} %all-gather.5.cloned.1.call-done, bf16[1024,1024]{1,0:T(8,128)(2,1)} %bitcast.2), kind=kOutput, calls=%fused_computation.4 | convolution fusion | flops 3758096384 | bytes 9437184 | tf_op jit(solution)/shard_map/dot_general | solution.py:124
  208.7 3.0 %fusion.1 = (bf16[1024,896]{0,1:T(8,128)(2,1)}, bf16[1024,896]{0,1:T(8,128)(2,1)}) fusion(bf16[1024,1792]{0,1:T(8,128)(2,1)S(1)} %convolution_bitcast_fusion, pred[1024,7]{0,1:T(8,128)(4,1)S(1)} %bitcast.76, pred[1024,7]{0,1:T(8,128)(4,1)S(1)} %bitcast.78), kind=kLoop, calls=%fused_computation.7 | loop fusion | flops 1835008 | bytes 7354368 | tf_op jit(solution)/shard_map/convert_element_type | solution.py:129
  211.7 3.8 %copy.26 = bf16[1024,896]{1,0:T(8,128)(2,1)} copy(bf16[1024,896]{0,1:T(8,128)(2,1)} %get-tuple-element.62) | data formatting | bytes 3670016
  215.5 3.8 %copy.25 = bf16[1024,896]{1,0:T(8,128)(2,1)} copy(bf16[1024,896]{0,1:T(8,128)(2,1)} %get-tuple-element.63) | data formatting | bytes 3670016
  219.3 7.2 %all-to-all-done.3 = bf16[16,64,1024]{2,1,0:T(8,128)(2,1)S(1)} async-done(((bf16[16,64,1024]{2,1,0:T(8,128)(2,1)}), bf16[16,64,1024]{2,1,0:T(8,128)(2,1)S(1)}, u32[]{:S(2)}, u32[]{:S(2)}) %all-to-all-start.3) | async-done | bytes 2097184 | tf_op jit(solution)/shard_map/all_to_all | solution.py:81
  226.5 1.1 reduce_sum.25
  (13 shorter events, 0.1 us)
Async XLA Ops:
  9.7 8.8 %copy-start.4 = (s32[8,7]{1,0:T(8,128)S(1)}, s32[8,7]{1,0:T(8,128)}, u32[]{:S(2)}) copy-start(s32[8,7]{1,0:T(8,128)} %param.16) | copy-start | bytes 676
  9.7 8.9 %copy-start.5 = (s32[8,7]{1,0:T(8,128)S(1)}, s32[8,7]{1,0:T(8,128)}, u32[]{:S(2)}) copy-start(s32[8,7]{1,0:T(8,128)} %param.17) | copy-start | bytes 676
  9.7 39.8 %all-to-all-start = ((bf16[16,64,1024]{2,1,0:T(8,128)(2,1)}), bf16[16,64,1024]{2,1,0:T(8,128)(2,1)}, u32[]{:S(2)}, u32[]{:S(2)}) async-start(bf16[16,64,1024]{2,1,0:T(8,128)(2,1)} %broadcast_in_dim.83), calls=%async_computation | async-start | bytes 4194304 | tf_op jit(solution)/shard_map/all_to_all | solution.py:88
  18.5 86.7 %reduce-scatter.2.cloned.1.call-start = ((), (), s32[]{:S(2)}) async-start(), calls=%async_computation.5 | async-start | bytes 8257536 | tf_op jit(solution)/shard_map/reduce_scatter | solution.py:32
  59.1 0.9 copy-start.3
  61.7 4.0 %copy-start.6 = (s32[7,8]{1,0:T(8,128)S(1)}, s32[7,8]{1,0:T(8,128)}, u32[]{:S(2)}) copy-start(s32[7,8]{1,0:T(8,128)} %param.18) | copy-start | bytes 676
  61.7 32.6 %all-to-all-start.1 = ((bf16[16,64,1024]{2,1,0:T(8,128)(2,1)}), bf16[16,64,1024]{2,1,0:T(8,128)(2,1)S(1)}, u32[]{:S(2)}, u32[]{:S(2)}) async-start(bf16[16,64,1024]{2,1,0:T(8,128)(2,1)} %broadcast_in_dim.84), calls=%async_computation.2 | async-start | bytes 4194304 | tf_op jit(solution)/shard_map/all_to_all | solution.py:88
  65.6 73.8 %all-gather.3.cloned.1.call-start = ((), (), s32[]{:S(2)}) async-start(), calls=%async_computation.6 | async-start | bytes 2064384 | tf_op jit(solution)/shard_map/all_gather | solution.py:38
  94.2 8.7 %copy-start.2 = (bf16[16,64,1024]{2,1,0:T(8,128)(2,1)}, bf16[16,64,1024]{2,1,0:T(8,128)(2,1)S(1)}, u32[]{:S(2)}) copy-start(bf16[16,64,1024]{2,1,0:T(8,128)(2,1)S(1)} %all-to-all-done.1) | copy-start | bytes 6291460
  107.1 70.3 %all-gather.5.cloned.1.call-start = ((), (), s32[]{:S(2)}) async-start(), calls=%async_computation.7 | async-start | bytes 4128768 | tf_op jit(solution)/shard_map/all_gather | solution.py:38
  110.6 5.9 %collective-permute-start = (bf16[4,128,896]{1,2,0:T(8,128)(2,1)}, bf16[4,128,896]{1,2,0:T(8,128)(2,1)}, u32[]{:S(2)}, u32[]{:S(2)}) collective-permute-start(bf16[4,128,896]{1,2,0:T(8,128)(2,1)} %bitcast_convert_fusion), channel_id=1, source_target_pairs={{0,16},{16,0},{32,48},{48,32},{64,80},{80,64},{96,112},{112,96},{1... | collective-permute-start | bytes 2752520 | tf_op jit(solution)/shard_map/ppermute | solution.py:60
  119.1 20.3 %copy-start.1 = (f32[128,1792]{0,1:T(8,128)S(1)}, f32[128,1792]{0,1:T(8,128)}, u32[]{:S(2)}) copy-start(f32[128,1792]{0,1:T(8,128)} %reduce-scatter.2.cloned.1.call-done) | copy-start | bytes 2752516
  119.2 11.5 %collective-permute-start.1 = (bf16[128,896]{0,1:T(8,128)(2,1)S(1)}, bf16[128,896]{0,1:T(8,128)(2,1)S(1)}, u32[]{:S(2)}, u32[]{:S(2)}) collective-permute-start(bf16[128,896]{0,1:T(8,128)(2,1)S(1)} %get-tuple-element.66), channel_id=1, source_target_pairs={{0,32},{16,48},{32,64},{48,80},{64,96},{80,112},{96,0},{112,16},{1... | collective-permute-start | bytes 688136 | tf_op jit(solution)/shard_map/ppermute | solution.py:66
  120.3 10.4 %collective-permute-start.3 = (bf16[128,896]{0,1:T(8,128)(2,1)S(1)}, bf16[128,896]{0,1:T(8,128)(2,1)S(1)}, u32[]{:S(2)}, u32[]{:S(2)}) collective-permute-start(bf16[128,896]{0,1:T(8,128)(2,1)S(1)} %get-tuple-element.67), channel_id=1, source_target_pairs={{0,96},{16,112},{32,0},{48,16},{64,32},{80,48},{96,64},{112,80},{1... | collective-permute-start | bytes 688136 | tf_op jit(solution)/shard_map/ppermute | solution.py:66
  121.9 16.3 %collective-permute-start.2 = (bf16[128,896]{0,1:T(8,128)(2,1)S(1)}, bf16[128,896]{0,1:T(8,128)(2,1)S(1)}, u32[]{:S(2)}, u32[]{:S(2)}) collective-permute-start(bf16[128,896]{0,1:T(8,128)(2,1)S(1)} %get-tuple-element.68), channel_id=1, source_target_pairs={{0,64},{16,80},{32,96},{48,112},{64,0},{80,16},{96,32},{112,48},{1... | collective-permute-start | bytes 688136 | tf_op jit(solution)/shard_map/ppermute | solution.py:66
  146.3 40.4 %all-to-all-start.2 = ((bf16[16,64,1024]{2,1,0:T(8,128)(2,1)}), bf16[16,64,1024]{2,1,0:T(8,128)(2,1)S(1)}, u32[]{:S(2)}, u32[]{:S(2)}) async-start(bf16[16,64,1024]{2,1,0:T(8,128)(2,1)} %bitcast.68), calls=%async_computation.3 | async-start | bytes 4194304 | tf_op jit(solution)/shard_map/all_to_all | solution.py:81
  186.7 1.3 copy-start
  188.0 38.5 %all-to-all-start.3 = ((bf16[16,64,1024]{2,1,0:T(8,128)(2,1)}), bf16[16,64,1024]{2,1,0:T(8,128)(2,1)S(1)}, u32[]{:S(2)}, u32[]{:S(2)}) async-start(bf16[16,64,1024]{2,1,0:T(8,128)(2,1)} %bitcast.67), calls=%async_computation.4 | async-start | bytes 4194304 | tf_op jit(solution)/shard_map/all_to_all | solution.py:81
Sparse Core Ops, SparseCore 0:
  59.3 45.7 reduce-scatter.1
  107.2 32.0 all-gather.2
  141.6 35.6 all-gather.4
where the time goes:
time: 235 us; the launch traced here: 234 us
  waiting for transfers between devices  97.3 us (41%)
  matrix products  42 us (18%)
  starting transfers between devices  31.8 us (14%)
  local copies, waits for them, and re-layouts  30.7 us (13%)
  other arithmetic  18.4 us (8%)
  between operations  13.9 us (6%)
    all_to_all x2, waiting for transfers between devices, group_gather(): pieces = lax.all_to_all(copies, ('col', 'depth'), 0, 0)  48.8 us
    all_gather x2, waiting for transfers between devices, row_gather(): return lax.all_gather(block, 'row', axis=0, tiled=True)  23.3 us
    unnamed x24, local copies, waits for them, and re-layouts  19.1 us
    ppermute x3, waiting for transfers between devices, row_sums_paired(): lax.ppermute(piece, 'row', [(i, (i + 2 * hop) % parts) for i in range(par...  15 us
    all_to_all x2, starting transfers between devices, group_sums(): lax.all_to_all(full.reshape((parts, rows) + full.shape[1:]), ('col', 'dep...  13.7 us
    all_to_all x2, starting transfers between devices, group_gather(): pieces = lax.all_to_all(copies, ('col', 'depth'), 0, 0)  12.7 us
    dot_general x1, matrix products, local(): hidden = jnp.dot(x_all, w_both, preferred_element_type=jnp.float32)  9.65 us
    dot_general x1, matrix products, input_term(): lax.dot_general(grads_all, w_both, outer, preferred_element_type=jnp.floa...  8.52 us
  transfers between devices with their start and end apart: 11, of which 8 were waited for; matrix products, arithmetic and copies ran while one was open for 31% of the time, Pallas kernels for 0%

commit v1 on v0

--- a/solution.py
+++ b/solution.py
@@ -1,9 +1,35 @@
+import functools
 import jax
 import jax.numpy as jnp
 from jax import lax
 from jax.sharding import PartitionSpec as P
 
 BLK = 128
+
+
+def replace_the_case(array_in, dim_at):
+    y = list(array_in.shape[1:])
+    y[dim_at] *= array_in.shape[0]
+    return jnp.moveaxis(array_in, 0, dim_at).reshape(y)
+
+
+def see_values_on(sample, along_axis, at_axis):
+    many = jax.lax.axis_size(along_axis)
+    by_place = [(q, (q + 1) % many) for q in range(many)]
+    lanes = [(dev_i, b) for b, dev_i in by_place]
+    spare, f_now = ([], [])
+    for pp in range(many - 1):
+        if pp % 2 == 0:
+            spare.append(jax.lax.ppermute(spare[-1] if spare else sample, along_axis, by_place))
+        else:
+            f_now.append(jax.lax.ppermute(f_now[-1] if f_now else sample, along_axis, lanes))
+    out_arr = jnp.stack([*spare[::-1], sample, *f_now], axis=0)
+    res = jax.lax.axis_index(along_axis) - len(spare)
+    out_arr = out_arr[(jnp.arange(many) - res) % many]
+    return replace_the_case(out_arr, at_axis)
+
+
+divide_the_series = functools.partial(see_values_on, along_axis="row", at_axis=0)
 
 
 def expand(mask):
@@ -35,7 +61,7 @@
 
 
 def row_gather(block):
-    return lax.all_gather(block, "row", axis=0, tiled=True)
+    return divide_the_series(block)
 
 
 def row_sums_direct(full):

time: 235 us -> 271 us (1.15)
  the two profiles are of different devices: /device:TPU:1 before, /device:TPU:3 now
where the time goes in v1:
time: 271 us; the launch traced here: 270 us
  waiting for transfers between devices  85.4 us (32%)
  local copies, waits for them, and re-layouts  62.9 us (23%)
  starting transfers between devices  48.7 us (18%)
  matrix products  41.5 us (15%)
  other arithmetic  17.1 us (6%)
  between operations  14.4 us (5%)
    all_to_all x2, waiting for transfers between devices, group_gather(): pieces = lax.all_to_all(copies, ('col', 'depth'), 0, 0)  48.8 us
    unnamed x60, local copies, waits for them, and re-layouts  34 us
    ppermute x8, waiting for transfers between devices, see_values_on(): jax.lax.ppermute(spare[-1] if spare else sample, along_axis, by_place)  22.1 us
    ppermute x8, starting transfers between devices, see_values_on(): jax.lax.ppermute(spare[-1] if spare else sample, along_axis, by_place)  16.8 us
    gather x4, local copies, waits for them, and re-layouts, see_values_on(): out_arr = out_arr[(jnp.arange(many) - res) % many]  15.8 us
    all_to_all x2, waiting for transfers between devices, group_sums(): lax.all_to_all(full.reshape((parts, rows) + full.shape[1:]), ('col', 'dep...  13.5 us
    all_to_all x2, starting transfers between devices, group_gather(): pieces = lax.all_to_all(copies, ('col', 'depth'), 0, 0)  11.9 us
    all_to_all x2, starting transfers between devices, group_sums(): lax.all_to_all(full.reshape((parts, rows) + full.shape[1:]), ('col', 'dep...  11.7 us
  transfers between devices with their start and end apart: 23, of which 10 were waited for; matrix products, arithmetic and copies ran while one was open for 36% of the time, Pallas kernels for 0%

profile of v1, /device:TPU:3, one launch (start us, length us, event | category | flops | bytes accessed | tf_op | source)
XLA Modules:
  0.0 270.1 jit_solution(11337239799262810410)
XLA Ops:
  7.2 2.5 broadcast_in_dim.85
  9.7 8.0 %all-to-all-start = ((bf16[16,64,1024]{2,1,0:T(8,128)(2,1)}), bf16[16,64,1024]{2,1,0:T(8,128)(2,1)}, u32[]{:S(2)}, u32[]{:S(2)}) async-start(bf16[16,64,1024]{2,1,0:T(8,128)(2,1)} %broadcast_in_dim.85), calls=%async_computation | async-start | bytes 4194304 | tf_op jit(solution)/shard_map/all_to_all | solution.py:114
  18.1 2.9 %copy.20 = bf16[1024,896]{0,1:T(8,128)(2,1)S(1)} copy(bf16[1024,896]{1,0:T(8,128)(2,1)} %param.13) | data formatting | bytes 3670016 | tf_op args[1]
  21.0 3.8 %copy.22 = bf16[1024,896]{0,1:T(8,128)(2,1)} copy(bf16[1024,896]{1,0:T(8,128)(2,1)} %param.14) | data formatting | bytes 3670016 | tf_op args[2]
  24.8 3.6 %bitcast_select_fusion.1 = (bf16[1024,896]{0,1:T(8,128)(2,1)}, bf16[1024,896]{0,1:T(8,128)(2,1)}) fusion(bf16[1024,896]{0,1:T(8,128)(2,1)} %copy.22, pred[1024,7]{0,1:T(8,128)(4,1)S(1)} %bitcast.117, bf16[1024,896]{0,1:T(8,128)(2,1)S(1)} %copy.20, pred[1024,7]{0,1:T(8,128)(4,1)S(1)} %bitcast.119), kind=kLoop, calls=%fused_computation.3 | loop fusion | flops 1835008 | bytes 7354368 | tf_op jit(solution)/shard_map/jit(_where)/select_n | solution.py:124
  28.4 20.2 %all-to-all-done = bf16[16,64,1024]{2,1,0:T(8,128)(2,1)} async-done(((bf16[16,64,1024]{2,1,0:T(8,128)(2,1)}), bf16[16,64,1024]{2,1,0:T(8,128)(2,1)}, u32[]{:S(2)}, u32[]{:S(2)}) %all-to-all-start) | async-done | bytes 2097184 | tf_op jit(solution)/shard_map/all_to_all | solution.py:114
  48.7 9.6 %convolution_bitcast_fusion.1 = f32[1024,1792]{0,1:T(8,128)} fusion(bf16[1024,1024]{1,0:T(8,128)(2,1)} %bitcast.2, bf16[1024,896]{0,1:T(8,128)(2,1)} %get-tuple-element.69, bf16[1024,896]{0,1:T(8,128)(2,1)} %get-tuple-element.70), kind=kOutput, calls=%fused_computation.7 | convolution fusion | flops 3765436416 | bytes 13107200 | tf_op jit(solution)/shard_map/dot_general | solution.py:133
  58.3 0.9 copy-done.15
  59.2 1.6 broadcast_in_dim.86
  60.8 3.9 %all-to-all-start.1 = ((bf16[16,64,1024]{2,1,0:T(8,128)(2,1)}), bf16[16,64,1024]{2,1,0:T(8,128)(2,1)S(1)}, u32[]{:S(2)}, u32[]{:S(2)}) async-start(bf16[16,64,1024]{2,1,0:T(8,128)(2,1)} %broadcast_in_dim.86), calls=%async_computation.2 | async-start | bytes 4194304 | tf_op jit(solution)/shard_map/all_to_all | solution.py:114
  64.8 28.6 %all-to-all-done.1 = bf16[16,64,1024]{2,1,0:T(8,128)(2,1)S(1)} async-done(((bf16[16,64,1024]{2,1,0:T(8,128)(2,1)}), bf16[16,64,1024]{2,1,0:T(8,128)(2,1)S(1)}, u32[]{:S(2)}, u32[]{:S(2)}) %all-to-all-start.1) | async-done | bytes 2097184 | tf_op jit(solution)/shard_map/all_to_all | solution.py:114
  93.4 2.8 %broadcast_in_dim.88 = pred[896,8,128]{2,1,0:T(8,128)(4,1)S(1)} broadcast(pred[896,8]{1,0:T(8,128)(4,1)S(1)} %bitcast.116), dimensions={0,1} | broadcast | bytes 924672 | tf_op jit(solution)/shard_map/broadcast_in_dim | solution.py:36
  96.2 0.9 copy-done.3
  97.2 5.9 %fusion.4 = f32[1024,896]{1,0:T(8,128)} fusion(bf16[1024,1024]{1,0:T(8,128)(2,1)S(1)} %bitcast.103, bf16[896,1024]{1,0:T(8,128)(2,1)} %param.15, pred[112,8,8,128]{3,2,1,0:T(8,128)(4,1)S(1)} %bitcast.113), kind=kOutput, calls=%fused_computation.18 | convolution fusion | flops 1879965696 | bytes 8519680 | tf_op jit(solution)/shard_map/dot_general | solution.py:137
  103.0 0.9 reduce-scatter.2.cloned.1.call-done
  104.0 1.6 constant_dynamic-slice_fusion
  106.2 1.1 bitcast_convert_fusion
  107.3 2.2 collective-permute-start.7
  109.7 1.1 collective-permute-start
  110.8 3.0 %collective-permute-done = bf16[128,896]{0,1:T(8,128)(2,1)S(1)} collective-permute-done((bf16[128,896]{0,1:T(8,128)(2,1)S(1)}, bf16[128,896]{0,1:T(8,128)(2,1)S(1)}, u32[]{:S(2)}, u32[]{:S(2)}) %collective-permute-start) | collective-permute-done | bytes 229408 | tf_op jit(solution)/shard_map/ppermute | solution.py:23
  113.8 2.5 collective-permute-start.1
  116.3 2.9 %collective-permute-done.1 = bf16[128,896]{0,1:T(8,128)(2,1)S(1)} collective-permute-done((bf16[128,896]{0,1:T(8,128)(2,1)S(1)}, bf16[128,896]{0,1:T(8,128)(2,1)S(1)}, u32[]{:S(2)}, u32[]{:S(2)}) %collective-permute-start.1) | collective-permute-done | bytes 229408 | tf_op jit(solution)/shard_map/ppermute | solution.py:23
  119.2 2.5 collective-permute-start.2
  121.7 2.9 %constant_dynamic-slice_fusion.1 = f32[4,1,128,896]{3,2,1,0:T(8,128)} fusion(f32[4,2,128,896]{3,2,1,0:T(8,128)} %bitcast.110, s32[]{:T(128)S(6)} %select_n.120), kind=kLoop, calls=%fused_computation.61 | loop fusion | bytes 3670020 | tf_op jit(solution)/shard_map/jit(_take) | solution.py:85
  124.6 1.8 copy.29
  126.4 1.7 collective-permute-start.3
  128.2 2.7 fusion.15
  130.9 1.0 collective-permute-start.8
  132.5 4.4 %collective-permute-start.9 = (bf16[128,896]{0,1:T(8,128)(2,1)S(1)}, bf16[128,896]{0,1:T(8,128)(2,1)}, u32[]{:S(2)}, u32[]{:S(2)}) collective-permute-start(bf16[128,896]{0,1:T(8,128)(2,1)S(1)} %get-tuple-element.68), channel_id=1, source_target_pairs={{0,64},{16,80},{32,96},{48,112},{64,0},{80,16},{96,32},{112,48},{1... | collective-permute-start | bytes 688136 | tf_op jit(solution)/shard_map/ppermute | solution.py:92
  137.6 1.6 bitcast_dynamic-update-slice_fusion.13
  140.7 0.8 bitcast_dynamic-update-slice_fusion.10
  142.2 1.6 bitcast_dynamic-update-slice_fusion.8
  144.5 2.4 gather_fusion
  147.0 2.6 copy.23
  149.6 1.5 fusion.8
  151.4 1.5 collective-permute-start.11
  152.9 5.4 %collective-permute-done.11 = bf16[128,1792]{0,1:T(8,128)(2,1)S(1)} collective-permute-done((bf16[128,1792]{0,1:T(8,128)(2,1)S(1)}, bf16[128,1792]{0,1:T(8,128)(2,1)S(1)}, u32[]{:S(2)}, u32[]{:S(2)}) %collective-permute-start.11) | collective-permute-done | bytes 458784 | tf_op jit(solution)/shard_map/ppermute | solution.py:23
  159.1 2.5 collective-permute-start.12
  161.6 5.4 %collective-permute-done.12 = bf16[128,1792]{0,1:T(8,128)(2,1)S(1)} collective-permute-done((bf16[128,1792]{0,1:T(8,128)(2,1)S(1)}, bf16[128,1792]{0,1:T(8,128)(2,1)S(1)}, u32[]{:S(2)}, u32[]{:S(2)}) %collective-permute-start.12) | collective-permute-done | bytes 458784 | tf_op jit(solution)/shard_map/ppermute | solution.py:23
  167.8 2.5 collective-permute-start.13
  170.3 5.4 %collective-permute-done.13 = bf16[128,1792]{0,1:T(8,128)(2,1)} collective-permute-done((bf16[128,1792]{0,1:T(8,128)(2,1)S(1)}, bf16[128,1792]{0,1:T(8,128)(2,1)}, u32[]{:S(2)}, u32[]{:S(2)}) %collective-permute-start.13) | collective-permute-done | bytes 458784 | tf_op jit(solution)/shard_map/ppermute | solution.py:23
  175.7 2.6 collective-permute-start.14
  178.3 5.3 %convolution_convert_fusion = bf16[1024,1024]{1,0:T(8,128)(2,1)} fusion(bf16[1024,896]{1,0:T(8,128)(2,1)S(1)} %bitcast.112, bf16[896,1024]{1,0:T(8,128)(2,1)} %param.15, pred[112,8,8,128]{3,2,1,0:T(8,128)(4,1)S(1)} %bitcast.114), kind=kOutput, calls=%fused_computation.15 | convolution fusion | flops 1881014272 | bytes 6684672 | tf_op jit(solution)/shard_map/dot_general | solution.py:142
  183.6 6.0 %all-to-all-start.2 = ((bf16[16,64,1024]{2,1,0:T(8,128)(2,1)}), bf16[16,64,1024]{2,1,0:T(8,128)(2,1)S(1)}, u32[]{:S(2)}, u32[]{:S(2)}) async-start(bf16[16,64,1024]{2,1,0:T(8,128)(2,1)} %bitcast.105), calls=%async_computation.3 | async-start | bytes 4194304 | tf_op jit(solution)/shard_map/all_to_all | solution.py:107
  189.7 1.9 bitcast_dynamic-update-slice_fusion.6
  191.6 1.8 bitcast_dynamic-update-slice_fusion.5
  193.4 0.8 bitcast_dynamic-update-slice_fusion.4
  195.0 0.8 maximum_dynamic-update-slice_fusion
  195.8 1.8 bitcast_dynamic-update-slice_fusion.2
  197.6 1.8 bitcast_dynamic-update-slice_fusion.1
  199.4 0.8 bitcast_dynamic-update-slice_fusion
  200.3 4.9 %gather_fusion.1 = bf16[8,128,1792]{1,2,0:T(8,128)(2,1)} fusion(bf16[8,128,1792]{1,2,0:T(8,128)(2,1)} %bitcast_dynamic-update-slice_fusion, s32[1024]{0:T(1024)S(1)} %pad_clamp_fusion), kind=kCustom, calls=%fused_computation.1 | custom fusion | bytes 7340064 | tf_op jit(solution)/shard_map/gather | solution.py:28
  205.1 5.9 %copy.26 = bf16[8,128,1792]{2,1,0:T(8,128)(2,1)} copy(bf16[8,128,1792]{1,2,0:T(8,128)(2,1)} %gather_fusion.1) | data formatting | bytes 7340032 | tf_op jit(solution)/shard_map/gather | solution.py:28
  211.0 8.4 %fusion.3 = bf16[1024,1024]{1,0:T(8,128)(2,1)} fusion(bf16[1024,1792]{1,0:T(8,128)(2,1)} %bitcast.101, bf16[1024,896]{0,1:T(8,128)(2,1)} %get-tuple-element.69, bf16[1024,896]{0,1:T(8,128)(2,1)} %get-tuple-element.70), kind=kOutput, calls=%fused_computation.14 | convolution fusion | flops 3766484992 | bytes 9437184 | tf_op jit(solution)/shard_map/dot_general | solution.py:158
  219.4 1.0 all-to-all-done.2
  220.5 5.7 %all-to-all-start.3 = ((bf16[16,64,1024]{2,1,0:T(8,128)(2,1)}), bf16[16,64,1024]{2,1,0:T(8,128)(2,1)}, u32[]{:S(2)}, u32[]{:S(2)}) async-start(bf16[16,64,1024]{2,1,0:T(8,128)(2,1)} %bitcast.106), calls=%async_computation.4 | async-start | bytes 4194304 | tf_op jit(solution)/shard_map/all_to_all | solution.py:107
  226.2 5.6 %select_convert_fusion = bf16[896,1024]{1,0:T(8,128)(2,1)} fusion(pred[112,8,8,128]{3,2,1,0:T(8,128)(4,1)S(1)} %bitcast.115, bf16[1024,896]{1,0:T(8,128)(2,1)} %bitcast.111, bf16[1024,1024]{1,0:T(8,128)(2,1)} %bitcast.104), kind=kOutput, calls=%fused_computation.11 | convolution fusion | flops 1880883200 | bytes 6684672 | tf_op jit(solution)/shard_map/dot_general | solution.py:145
  231.8 1.1 reduce_sum.24
  232.8 6.7 %convolution_bitcast_fusion = bf16[1024,1792]{0,1:T(8,128)(2,1)S(1)} fusion(bf16[1024,1792]{1,0:T(8,128)(2,1)} %bitcast.102, bf16[1024,1024]{1,0:T(8,128)(2,1)} %bitcast.2), kind=kOutput, calls=%fused_computation.6 | convolution fusion | flops 3758096384 | bytes 9437184 | tf_op jit(solution)/shard_map/dot_general | solution.py:150
  239.6 2.3 fusion.1
  241.9 3.8 %copy.28 = bf16[1024,896]{1,0:T(8,128)(2,1)} copy(bf16[1024,896]{0,1:T(8,128)(2,1)} %get-tuple-element.62) | data formatting | bytes 3670016
  245.7 2.4 copy.27
  248.1 12.4 %all-to-all-done.3 = bf16[16,64,1024]{2,1,0:T(8,128)(2,1)} async-done(((bf16[16,64,1024]{2,1,0:T(8,128)(2,1)}), bf16[16,64,1024]{2,1,0:T(8,128)(2,1)}, u32[]{:S(2)}, u32[]{:S(2)}) %all-to-all-start.3) | async-done | bytes 2097184 | tf_op jit(solution)/shard_map/all_to_all | solution.py:107
  260.5 2.7 reduce_sum.25
  (81 shorter events, 8.2 us)
Async XLA Ops:
  9.7 8.0 %copy-start.16 = (s32[8,7]{1,0:T(8,128)S(1)}, s32[8,7]{1,0:T(8,128)}, u32[]{:S(2)}) copy-start(s32[8,7]{1,0:T(8,128)} %param.16) | copy-start | bytes 676
  9.7 8.1 %copy-start.17 = (s32[8,7]{1,0:T(8,128)S(1)}, s32[8,7]{1,0:T(8,128)}, u32[]{:S(2)}) copy-start(s32[8,7]{1,0:T(8,128)} %param.17) | copy-start | bytes 676
  9.7 39.0 %all-to-all-start = ((bf16[16,64,1024]{2,1,0:T(8,128)(2,1)}), bf16[16,64,1024]{2,1,0:T(8,128)(2,1)}, u32[]{:S(2)}, u32[]{:S(2)}) async-start(bf16[16,64,1024]{2,1,0:T(8,128)(2,1)} %broadcast_in_dim.85), calls=%async_computation | async-start | bytes 4194304 | tf_op jit(solution)/shard_map/all_to_all | solution.py:114
  17.7 86.3 %reduce-scatter.2.cloned.1.call-start = ((), (), s32[]{:S(2)}) async-start(), calls=%async_computation.5 | async-start | bytes 8257536 | tf_op jit(solution)/shard_map/reduce_scatter | solution.py:58
  58.3 0.9 copy-start.15
  60.8 4.0 %copy-start.18 = (s32[7,8]{1,0:T(8,128)S(1)}, s32[7,8]{1,0:T(8,128)}, u32[]{:S(2)}) copy-start(s32[7,8]{1,0:T(8,128)} %param.18) | copy-start | bytes 676
  60.8 32.6 %all-to-all-start.1 = ((bf16[16,64,1024]{2,1,0:T(8,128)(2,1)}), bf16[16,64,1024]{2,1,0:T(8,128)(2,1)S(1)}, u32[]{:S(2)}, u32[]{:S(2)}) async-start(bf16[16,64,1024]{2,1,0:T(8,128)(2,1)} %broadcast_in_dim.86), calls=%async_computation.2 | async-start | bytes 4194304 | tf_op jit(solution)/shard_map/all_to_all | solution.py:114
  93.4 9.6 %copy-start.1 = (bf16[16,64,1024]{2,1,0:T(8,128)(2,1)}, bf16[16,64,1024]{2,1,0:T(8,128)(2,1)S(1)}, u32[]{:S(2)}) copy-start(bf16[16,64,1024]{2,1,0:T(8,128)(2,1)S(1)} %all-to-all-done.1) | copy-start | bytes 6291460
  96.2 0.9 copy-start.3
  105.6 4.0 %copy-start = (f32[128,1792]{0,1:T(8,128)S(1)}, f32[128,1792]{0,1:T(8,128)}, u32[]{:S(2)}) copy-start(f32[128,1792]{0,1:T(8,128)} %reduce-scatter.2.cloned.1.call-done) | copy-start | bytes 2752516
  107.3 20.8 %collective-permute-start.7 = (bf16[4,128,896]{1,2,0:T(8,128)(2,1)}, bf16[4,128,896]{1,2,0:T(8,128)(2,1)}, u32[]{:S(2)}, u32[]{:S(2)}) collective-permute-start(bf16[4,128,896]{1,2,0:T(8,128)(2,1)} %bitcast_convert_fusion), channel_id=1, source_target_pairs={{0,16},{16,0},{32,48},{48,32},{64,80},{80,64},{96,112},{112,96},{1... | collective-permute-start | bytes 2752520 | tf_op jit(solution)/shard_map/ppermute | solution.py:86
  109.7 4.1 %collective-permute-start = (bf16[128,896]{0,1:T(8,128)(2,1)S(1)}, bf16[128,896]{0,1:T(8,128)(2,1)S(1)}, u32[]{:S(2)}, u32[]{:S(2)}) collective-permute-start(bf16[128,896]{0,1:T(8,128)(2,1)S(1)} %multiply_convert_fusion.2), channel_id=1, source_target_pairs={{0,16},{16,32},{32,48},{48,64},{64,80},{80,96},{96,112},{112,0},{1... | collective-permute-start | bytes 688136 | tf_op jit(solution)/shard_map/ppermute | solution.py:23
  110.8 5.5 %collective-permute-start.4 = (bf16[128,896]{0,1:T(8,128)(2,1)S(1)}, bf16[128,896]{0,1:T(8,128)(2,1)S(1)}, u32[]{:S(2)}, u32[]{:S(2)}) collective-permute-start(bf16[128,896]{0,1:T(8,128)(2,1)S(1)} %multiply_convert_fusion.2), channel_id=1, source_target_pairs={{16,0},{32,16},{48,32},{64,48},{80,64},{96,80},{112,96},{0,112},{1... | collective-permute-start | bytes 688136 | tf_op jit(solution)/shard_map/ppermute | solution.py:25
  113.8 7.9 %copy-start.11 = (bf16[128,896]{0,1:T(8,128)(2,1)}, bf16[128,896]{0,1:T(8,128)(2,1)S(1)}, u32[]{:S(2)}) copy-start(bf16[128,896]{0,1:T(8,128)(2,1)S(1)} %collective-permute-done) | copy-start | bytes 688132
  113.8 5.4 %collective-permute-start.1 = (bf16[128,896]{0,1:T(8,128)(2,1)S(1)}, bf16[128,896]{0,1:T(8,128)(2,1)S(1)}, u32[]{:S(2)}, u32[]{:S(2)}) collective-permute-start(bf16[128,896]{0,1:T(8,128)(2,1)S(1)} %collective-permute-done), channel_id=1, source_target_pairs={{0,16},{16,32},{32,48},{48,64},{64,80},{80,96},{96,112},{112,0},{1... | collective-permute-start | bytes 688136 | tf_op jit(solution)/shard_map/ppermute | solution.py:23
  116.3 10.1 %copy-start.9 = (bf16[128,896]{0,1:T(8,128)(2,1)}, bf16[128,896]{0,1:T(8,128)(2,1)S(1)}, u32[]{:S(2)}) copy-start(bf16[128,896]{0,1:T(8,128)(2,1)S(1)} %collective-permute-done.4) | copy-start | bytes 688132
  116.3 10.1 %collective-permute-start.5 = (bf16[128,896]{0,1:T(8,128)(2,1)S(1)}, bf16[128,896]{0,1:T(8,128)(2,1)}, u32[]{:S(2)}, u32[]{:S(2)}) collective-permute-start(bf16[128,896]{0,1:T(8,128)(2,1)S(1)} %collective-permute-done.4), channel_id=1, source_target_pairs={{16,0},{32,16},{48,32},{64,48},{80,64},{96,80},{112,96},{0,112},{1... | collective-permute-start | bytes 688136 | tf_op jit(solution)/shard_map/ppermute | solution.py:25
  119.2 7.2 %copy-start.13 = (bf16[128,896]{0,1:T(8,128)(2,1)}, bf16[128,896]{0,1:T(8,128)(2,1)S(1)}, u32[]{:S(2)}) copy-start(bf16[128,896]{0,1:T(8,128)(2,1)S(1)} %collective-permute-done.1) | copy-start | bytes 688132
  119.2 7.2 %collective-permute-start.2 = (bf16[128,896]{0,1:T(8,128)(2,1)S(1)}, bf16[128,896]{0,1:T(8,128)(2,1)}, u32[]{:S(2)}, u32[]{:S(2)}) collective-permute-start(bf16[128,896]{0,1:T(8,128)(2,1)S(1)} %collective-permute-done.1), channel_id=1, source_target_pairs={{0,16},{16,32},{32,48},{48,64},{64,80},{80,96},{96,112},{112,0},{1... | collective-permute-start | bytes 688136 | tf_op jit(solution)/shard_map/ppermute | solution.py:23
  126.4 17.4 %collective-permute-start.6 = (bf16[128,896]{0,1:T(8,128)(2,1)}, bf16[128,896]{0,1:T(8,128)(2,1)S(1)}, u32[]{:S(2)}, u32[]{:S(2)}) collective-permute-start(bf16[128,896]{0,1:T(8,128)(2,1)} %collective-permute-done.5), channel_id=1, source_target_pairs={{16,0},{32,16},{48,32},{64,48},{80,64},{96,80},{112,96},{0,112},{1... | collective-permute-start | bytes 688136 | tf_op jit(solution)/shard_map/ppermute | solution.py:25
  126.4 10.5 %collective-permute-start.3 = (bf16[128,896]{0,1:T(8,128)(2,1)}, bf16[128,896]{0,1:T(8,128)(2,1)S(1)}, u32[]{:S(2)}, u32[]{:S(2)}) collective-permute-start(bf16[128,896]{0,1:T(8,128)(2,1)} %collective-permute-done.2), channel_id=1, source_target_pairs={{0,16},{16,32},{32,48},{48,64},{64,80},{80,96},{96,112},{112,0},{1... | collective-permute-start | bytes 688136 | tf_op jit(solution)/shard_map/ppermute | solution.py:23
  130.9 8.4 %copy-start.14 = (bf16[128,896]{0,1:T(8,128)(2,1)S(1)}, bf16[128,896]{0,1:T(8,128)(2,1)}, u32[]{:S(2)}) copy-start(bf16[128,896]{0,1:T(8,128)(2,1)} %copy-done.13) | copy-start | bytes 688132
  130.9 9.1 %copy-start.12 = (bf16[128,896]{0,1:T(8,128)(2,1)S(1)}, bf16[128,896]{0,1:T(8,128)(2,1)}, u32[]{:S(2)}) copy-start(bf16[128,896]{0,1:T(8,128)(2,1)} %copy-done.11) | copy-start | bytes 688132
  130.9 10.6 %copy-start.10 = (bf16[128,896]{0,1:T(8,128)(2,1)S(1)}, bf16[128,896]{0,1:T(8,128)(2,1)}, u32[]{:S(2)}) copy-start(bf16[128,896]{0,1:T(8,128)(2,1)} %copy-done.9) | copy-start | bytes 688132
  130.9 18.7 %collective-permute-start.8 = (bf16[128,896]{0,1:T(8,128)(2,1)S(1)}, bf16[128,896]{0,1:T(8,128)(2,1)}, u32[]{:S(2)}, u32[]{:S(2)}) collective-permute-start(bf16[128,896]{0,1:T(8,128)(2,1)S(1)} %get-tuple-element.66), channel_id=1, source_target_pairs={{0,32},{16,48},{32,64},{48,80},{64,96},{80,112},{96,0},{112,16},{1... | collective-permute-start | bytes 688136 | tf_op jit(solution)/shard_map/ppermute | solution.py:92
  132.0 17.6 %collective-permute-start.10 = (bf16[128,896]{0,1:T(8,128)(2,1)S(1)}, bf16[128,896]{0,1:T(8,128)(2,1)}, u32[]{:S(2)}, u32[]{:S(2)}) collective-permute-start(bf16[128,896]{0,1:T(8,128)(2,1)S(1)} %get-tuple-element.67), channel_id=1, source_target_pairs={{0,96},{16,112},{32,0},{48,16},{64,32},{80,48},{96,64},{112,80},{1... | collective-permute-start | bytes 688136 | tf_op jit(solution)/shard_map/ppermute | solution.py:92
  132.5 17.1 %collective-permute-start.9 = (bf16[128,896]{0,1:T(8,128)(2,1)S(1)}, bf16[128,896]{0,1:T(8,128)(2,1)}, u32[]{:S(2)}, u32[]{:S(2)}) collective-permute-start(bf16[128,896]{0,1:T(8,128)(2,1)S(1)} %get-tuple-element.68), channel_id=1, source_target_pairs={{0,64},{16,80},{32,96},{48,112},{64,0},{80,16},{96,32},{112,48},{1... | collective-permute-start | bytes 688136 | tf_op jit(solution)/shard_map/ppermute | solution.py:92
  149.6 28.7 %copy-start.2 = (bf16[8,128,896]{2,1,0:T(8,128)(2,1)S(1)}, bf16[8,128,896]{2,1,0:T(8,128)(2,1)}, u32[]{:S(2)}) copy-start(bf16[8,128,896]{2,1,0:T(8,128)(2,1)} %copy.23) | copy-start | bytes 5505028
  149.6 28.7 %copy-start.4 = (pred[896,8,128]{2,1,0:T(8,128)(4,1)S(1)}, pred[896,8,128]{2,1,0:T(8,128)(4,1)}, u32[]{:S(2)}) copy-start(pred[896,8,128]{2,1,0:T(8,128)(4,1)} %copy-done.3) | copy-start | bytes 2752516
  151.4 6.9 %collective-permute-start.11 = (bf16[128,1792]{0,1:T(8,128)(2,1)S(1)}, bf16[128,1792]{0,1:T(8,128)(2,1)S(1)}, u32[]{:S(2)}, u32[]{:S(2)}) collective-permute-start(bf16[128,1792]{0,1:T(8,128)(2,1)S(1)} %pad_maximum_fusion.5), channel_id=1, source_target_pairs={{0,16},{16,32},{32,48},{48,64},{64,80},{80,96},{96,112},{112,0},{1... | collective-permute-start | bytes 1376264 | tf_op jit(solution)/shard_map/ppermute | solution.py:23
  158.3 0.8 copy-start.5
  159.1 7.9 %collective-permute-start.12 = (bf16[128,1792]{0,1:T(8,128)(2,1)S(1)}, bf16[128,1792]{0,1:T(8,128)(2,1)S(1)}, u32[]{:S(2)}, u32[]{:S(2)}) collective-permute-start(bf16[128,1792]{0,1:T(8,128)(2,1)S(1)} %collective-permute-done.11), channel_id=1, source_target_pairs={{0,16},{16,32},{32,48},{48,64},{64,80},{80,96},{96,112},{112,0},{1... | collective-permute-start | bytes 1376264 | tf_op jit(solution)/shard_map/ppermute | solution.py:23
  161.6 8.7 %collective-permute-start.15 = (bf16[128,1792]{0,1:T(8,128)(2,1)S(1)}, bf16[128,1792]{0,1:T(8,128)(2,1)}, u32[]{:S(2)}, u32[]{:S(2)}) collective-permute-start(bf16[128,1792]{0,1:T(8,128)(2,1)S(1)} %pad_maximum_fusion.5), channel_id=1, source_target_pairs={{16,0},{32,16},{48,32},{64,48},{80,64},{96,80},{112,96},{0,112},{1... | collective-permute-start | bytes 1376264 | tf_op jit(solution)/shard_map/ppermute | solution.py:25
  167.0 0.8 copy-start.7
  167.8 7.9 %collective-permute-start.13 = (bf16[128,1792]{0,1:T(8,128)(2,1)S(1)}, bf16[128,1792]{0,1:T(8,128)(2,1)}, u32[]{:S(2)}, u32[]{:S(2)}) collective-permute-start(bf16[128,1792]{0,1:T(8,128)(2,1)S(1)} %collective-permute-done.12), channel_id=1, source_target_pairs={{0,16},{16,32},{32,48},{48,64},{64,80},{80,96},{96,112},{112,0},{1... | collective-permute-start | bytes 1376264 | tf_op jit(solution)/shard_map/ppermute | solution.py:23
  170.3 19.3 %collective-permute-start.16 = (bf16[128,1792]{0,1:T(8,128)(2,1)}, bf16[128,1792]{0,1:T(8,128)(2,1)}, u32[]{:S(2)}, u32[]{:S(2)}) collective-permute-start(bf16[128,1792]{0,1:T(8,128)(2,1)} %collective-permute-done.15), channel_id=1, source_target_pairs={{16,0},{32,16},{48,32},{64,48},{80,64},{96,80},{112,96},{0,112},{1... | collective-permute-start | bytes 1376264 | tf_op jit(solution)/shard_map/ppermute | solution.py:25
  175.7 13.9 %collective-permute-start.14 = (bf16[128,1792]{0,1:T(8,128)(2,1)}, bf16[128,1792]{0,1:T(8,128)(2,1)}, u32[]{:S(2)}, u32[]{:S(2)}) collective-permute-start(bf16[128,1792]{0,1:T(8,128)(2,1)} %collective-permute-done.13), channel_id=1, source_target_pairs={{0,16},{16,32},{32,48},{48,64},{64,80},{80,96},{96,112},{112,0},{1... | collective-permute-start | bytes 1376264 | tf_op jit(solution)/shard_map/ppermute | solution.py:23
  183.6 36.9 %all-to-all-start.2 = ((bf16[16,64,1024]{2,1,0:T(8,128)(2,1)}), bf16[16,64,1024]{2,1,0:T(8,128)(2,1)S(1)}, u32[]{:S(2)}, u32[]{:S(2)}) async-start(bf16[16,64,1024]{2,1,0:T(8,128)(2,1)} %bitcast.105), calls=%async_computation.3 | async-start | bytes 4194304 | tf_op jit(solution)/shard_map/all_to_all | solution.py:107
  189.6 3.8 %copy-start.8 = (bf16[128,1792]{0,1:T(8,128)(2,1)S(1)}, bf16[128,1792]{0,1:T(8,128)(2,1)}, u32[]{:S(2)}) copy-start(bf16[128,1792]{0,1:T(8,128)(2,1)} %copy-done.7) | copy-start | bytes 1376260
  189.6 4.6 %copy-start.6 = (bf16[128,1792]{0,1:T(8,128)(2,1)S(1)}, bf16[128,1792]{0,1:T(8,128)(2,1)}, u32[]{:S(2)}) copy-start(bf16[128,1792]{0,1:T(8,128)(2,1)} %copy-done.5) | copy-start | bytes 1376260
  189.6 9.8 %collective-permute-start.17 = (bf16[128,1792]{0,1:T(8,128)(2,1)}, bf16[128,1792]{0,1:T(8,128)(2,1)S(1)}, u32[]{:S(2)}, u32[]{:S(2)}) collective-permute-start(bf16[128,1792]{0,1:T(8,128)(2,1)} %collective-permute-done.16), channel_id=1, source_target_pairs={{16,0},{32,16},{48,32},{64,48},{80,64},{96,80},{112,96},{0,112},{1... | collective-permute-start | bytes 1376264 | tf_op jit(solution)/shard_map/ppermute | solution.py:25
  220.5 40.1 %all-to-all-start.3 = ((bf16[16,64,1024]{2,1,0:T(8,128)(2,1)}), bf16[16,64,1024]{2,1,0:T(8,128)(2,1)}, u32[]{:S(2)}, u32[]{:S(2)}) async-start(bf16[16,64,1024]{2,1,0:T(8,128)(2,1)} %bitcast.106), calls=%async_computation.4 | async-start | bytes 4194304 | tf_op jit(solution)/shard_map/all_to_all | solution.py:107
Sparse Core Ops, SparseCore 0:
  58.4 45.4 reduce-scatter.1
